TPU v7x, 32 devices: a whole 2x2x4 slice. The times are simulated.
32 devices in a mesh: tract: 2 (over x), skyx: 4 (over y, core), skyy: 4 (over z).
Axes of the slice: x: 2, y: 2, z: 4, core: 2. Of those that a mesh axis runs over, the one named last changes fastest.
Arguments:
- images: bfloat16 [8, 8, 136, 4480], P(('tract', 'skyy'), 'skyx'), parts along dimension 0, may hold values from -6 to 6
- masks: int32 [8, 8, 136, 4480], P(('tract', 'skyy'), 'skyx'), parts along dimension 0, may hold values 0 or 1
- row_kernels: bfloat16 [8, 8, 128, 136], P(('tract', 'skyy'), 'skyx'), parts along dimension 0, may hold values from -1 to 2
- col_kernel: bfloat16 [66, 384, 128], P('tract'), parts along dimension 0, may hold values from -1 to 2
- inv_var: float32 [8, 8], P(('tract', 'skyy')), parts along dimension 0, may hold values from 0.5 to 4
- dest_col: int32 [8, 128, 1], P(('tract', 'skyy'), 'skyx'), parts along dimension 0, may hold values from 0 to 3; in each aligned block of 32 rows (0 to 31, 32 to 63, ..., all dimensions but the last counted through in order) at most 12 rows name the same one
- dest_row: int32 [8, 128], P(('tract', 'skyy'), 'skyx'), parts along dimension 0, may hold values from 0 to 31
Outputs:
- coadd: float32 [1024, 15872], P(('tract', 'skyy'), 'skyx'), parts along dimension 0
There are 2 independent parts, one for each index of `tract`. A program takes and returns all parts, laid end to end along the dimension named above; each array names one. Nothing has to cross between parts.
Inputs may be any that keep to these rules, and one draw needn't show every extreme that they name: `dest_col`: the 32 row blocks of any one device name one patch column at most 12 times, and some device names one exactly 12 times.
All inputs are finite; a program needn't handle non-finite values. No bound on the sum of `masks` on one device may be relied on, other than what follows from the above.
Results may differ from a plain program's by a relative error of at most 0.0057.
Values may be sent and summed in bfloat16 or wider, within the bound.
No kernel may reach another device: no remote copies, remote signals or barrier semaphores. Data moves between devices by JAX's collectives and lax.ppermute only.
A program may use at most 128 MiB of HBM per device.

v0:
```python
import jax
import jax.numpy as jnp
from jax import lax
from jax.experimental import pallas as pl
from jax.experimental.pallas import tpu as pltpu
from jax.sharding import PartitionSpec as P


OVY = 64
PR = 128
RB = 8
SPLIT = (5, 11, 11, 6)
ROW_PIECE = 640


def shifted(value, axis, steps):
    count = lax.axis_size(axis)
    first, last = (max(0, -steps), min(count, count - steps))
    return lax.ppermute(value, axis, [(source, source + steps) for source in range(first, last)])


def make_warp_kernel(start, width, first_tile, exposures):
    def kernel(w_ref, idx_ref, img_hbm, mask_hbm, rk_ref, ck_hbm, prev_ref, out_ref, img_buf, mask_buf, rw_buf, blk_buf, ck_ref, sems):
        ph = rk_ref.shape[2]
        tiles, kw, tw = ck_ref.shape
        blocks = ph // RB
        ck_copy = pltpu.make_async_copy(ck_hbm.at[pl.ds(first_tile, tiles)], ck_ref, sems.at[2, 0])
        ck_copy.start()
        copies = []
        for e in range(exposures):
            ci = pltpu.make_async_copy(img_hbm.at[0, e, :, pl.ds(start, width)], img_buf.at[e], sems.at[0, e])
            cm = pltpu.make_async_copy(mask_hbm.at[0, e, :, pl.ds(start, width)], mask_buf.at[e], sems.at[1, e])
            ci.start()
            cm.start()
            copies.append((ci, cm))
        for e in range(exposures):
            ci, cm = copies[e]
            ci.wait()
            cm.wait()
            rk = rk_ref[0, e]
            if e == 0:
                ck_copy.wait()
            piece_start = 0
            while piece_start < width:
                piece = min(ROW_PIECE, width - piece_start)
                cols = pl.ds(piece_start, piece)
                good = mask_buf[e, :, cols] == 0
                img = img_buf[e, :, cols]
                p0 = jnp.where(good, img, jnp.zeros_like(img))
                p1 = good.astype(jnp.bfloat16)
                rw_buf[0:ph, cols] = jnp.dot(rk, p0, preferred_element_type=jnp.float32).astype(jnp.bfloat16)
                rw_buf[ph : 2 * ph, cols] = jnp.dot(rk, p1, preferred_element_type=jnp.float32).astype(jnp.bfloat16)
                piece_start += piece
            weight = w_ref[e]

            def tile(t, carry):
                off = pl.multiple_of(t * tw, tw)
                x = rw_buf[:, pl.ds(off, kw)]
                r = jnp.dot(x, ck_ref[t], preferred_element_type=jnp.float32) * weight
                rows = pl.ds(e * blocks, blocks)
                blk_buf[rows, 0, :, pl.ds(off, tw)] = r[0:ph].reshape(blocks, RB, tw).astype(jnp.bfloat16)
                blk_buf[rows, 1, :, pl.ds(off, tw)] = r[ph : 2 * ph].reshape(blocks, RB, tw).astype(jnp.bfloat16)
                return carry

            lax.fori_loop(0, tiles, tile, 0)

        def gather(slot, carry):
            out_ref[slot] = blk_buf[idx_ref[slot]]
            return carry

        lax.fori_loop(0, out_ref.shape[0], gather, 0)

    return kernel


def warp_chunk(first_tile, per, weights, send_idx, images, masks, row_kernels, col_kernel, previous):
    _, exposures, hin, _ = images.shape
    ph = row_kernels.shape[2]
    _, kw, tw = col_kernel.shape
    width = per * tw
    window = width + kw - tw
    start = first_tile * tw
    blocks = ph // RB
    slots = send_idx.shape[0]
    return pl.pallas_call(
        make_warp_kernel(start, window, first_tile, exposures),
        in_specs=[
            pl.BlockSpec(memory_space=pltpu.SMEM),
            pl.BlockSpec(memory_space=pltpu.SMEM),
            pl.BlockSpec(memory_space=pl.ANY),
            pl.BlockSpec(memory_space=pl.ANY),
            pl.BlockSpec(memory_space=pltpu.VMEM),
            pl.BlockSpec(memory_space=pl.ANY),
            pl.BlockSpec(memory_space=pl.ANY),
        ],
        out_specs=pl.BlockSpec(memory_space=pltpu.VMEM),
        out_shape=jax.ShapeDtypeStruct((slots, 2, RB, width), jnp.bfloat16),
        scratch_shapes=[
            pltpu.VMEM((exposures, hin, window), jnp.bfloat16),
            pltpu.VMEM((exposures, hin, window), jnp.int32),
            pltpu.VMEM((2 * ph, window), jnp.bfloat16),
            pltpu.VMEM((exposures * blocks, 2, RB, width), jnp.bfloat16),
            pltpu.VMEM((per, kw, tw), jnp.bfloat16),
            pltpu.SemaphoreType.DMA((3, exposures)),
        ],
        compiler_params=pltpu.CompilerParams(vmem_limit_bytes=48 * 1024 * 1024),
        cost_estimate=pl.CostEstimate(
            flops=exposures * (8 * ph * hin * window + 4 * ph * kw * width),
            transcendentals=0,
            bytes_accessed=exposures * hin * window * 6 + per * kw * tw * 2 + slots * 2 * RB * width * 2,
        ),
    )(weights, send_idx, images, masks, row_kernels, col_kernel, previous)


def make_place_kernel(groups, capacity, positions, margin, inner):
    def kernel(rows_ref, *refs):
        recv_refs = refs[:groups]
        upper_ref, lower_ref, int_ref, canvas = refs[-4:]
        canvas[...] = jnp.zeros(canvas.shape, jnp.float32)
        for g in range(groups):
            def body(c, carry, g=g):
                pos = rows_ref[g * capacity + c]

                @pl.when((pos >= 0) & (pos < positions))
                def _():
                    canvas[pos] += recv_refs[g][c].astype(jnp.float32)

                return carry

            lax.fori_loop(0, capacity, body, 0)
        upper_ref[...] = canvas[0:margin].astype(jnp.bfloat16)
        lower_ref[...] = canvas[margin + inner :].astype(jnp.bfloat16)
        int_ref[...] = canvas[margin : margin + inner]

    return kernel


def place(rows, recvs, after, positions, margin, inner):
    after = list(after)
    groups = len(recvs)
    capacity = recvs[0].shape[0]
    block = recvs[0].shape[1:]
    return pl.pallas_call(
        make_place_kernel(groups, capacity, positions, margin, inner),
        in_specs=[pl.BlockSpec(memory_space=pltpu.SMEM)]
        + [pl.BlockSpec(memory_space=pltpu.VMEM)] * groups
        + [pl.BlockSpec(memory_space=pl.ANY)] * len(after),
        out_specs=[pl.BlockSpec(memory_space=pltpu.VMEM)] * 3,
        out_shape=[
            jax.ShapeDtypeStruct((margin,) + block, jnp.bfloat16),
            jax.ShapeDtypeStruct((margin,) + block, jnp.bfloat16),
            jax.ShapeDtypeStruct((inner,) + block, jnp.float32),
        ],
        scratch_shapes=[pltpu.VMEM((positions,) + block, jnp.float32)],
        compiler_params=pltpu.CompilerParams(vmem_limit_bytes=32 * 1024 * 1024),
    )(rows, *recvs, *after)


def local_body(images, masks, row_kernels, col_kernel, inv_var, dest_col, dest_row):
    exposures = images.shape[1]
    tile_width = col_kernel.shape[2]
    cw = col_kernel.shape[0] * tile_width
    pw = cw - 2 * tile_width
    tiles = col_kernel.shape[0]
    bounds = [tiles * sum(SPLIT[:i]) // sum(SPLIT) for i in range(len(SPLIT) + 1)]
    first_exp = lax.axis_index("skyx") * exposures
    weights = lax.dynamic_slice_in_dim(inv_var[0], first_exp, exposures)

    slot_dest = dest_col[0, :, 0]
    slot_rows = dest_row[0]
    slot_count = slot_dest.shape[0]
    peers = lax.axis_size("skyx")
    capacity = max(2, (3 * slot_count + 2 * peers - 1) // (2 * peers))
    positions = (PR + 2 * OVY) // RB
    offsets = (slot_dest - lax.axis_index("skyx")) % peers
    earlier = (jnp.arange(slot_count)[None, :] < jnp.arange(slot_count)[:, None]).astype(jnp.int32)
    onehot_dest = (offsets[:, None] == jnp.arange(peers)[None, :]).astype(jnp.int32)
    ranks = jnp.sum(jnp.dot(earlier, onehot_dest) * onehot_dest, axis=1)
    chosen = (offsets[None, None, :] == jnp.arange(peers)[:, None, None]) & (
        ranks[None, None, :] == jnp.arange(capacity)[None, :, None]
    )
    send_rows = jnp.sum(jnp.where(chosen, slot_rows[None, None, :] + 1, 0), axis=2) - 1
    send_idx = jnp.sum(jnp.where(chosen, jnp.arange(slot_count)[None, None, :] + 1, 0), axis=2) - 1
    send_idx = jnp.clip(send_idx, 0, slot_count - 1).reshape(-1)
    rings = [[(i, (i + step) % peers) for i in range(peers)] for step in range(peers)]
    table = lax.all_gather(jnp.stack([slot_dest, slot_rows]), "skyx")
    mine = (table[:, 0] == lax.axis_index("skyx")).astype(jnp.int32)
    mine_rank = jnp.dot(mine, earlier.T)
    picked = (mine[:, None, :] == 1) & (mine_rank[:, None, :] == jnp.arange(capacity)[None, :, None])
    recv_from = jnp.sum(jnp.where(picked, table[:, 1][:, None, :] + 1, 0), axis=2)
    sources = (lax.axis_index("skyx") - jnp.arange(peers)) % peers
    by_step = sources[:, None] == jnp.arange(peers)[None, :]
    recv_rows = jnp.sum(jnp.where(by_step[:, :, None], recv_from[None, :, :], 0), axis=1) - 1
    recv_rows = recv_rows.reshape(-1)

    margin = OVY // RB
    inner = PR // RB
    interiors = []
    after = [recv_rows]
    previous = recv_rows
    for chunk in range(len(SPLIT)):
        per = bounds[chunk + 1] - bounds[chunk]
        send_buf = warp_chunk(bounds[chunk], per, weights, send_idx, images, masks, row_kernels, col_kernel, previous)
        previous = send_buf
        send_buf = send_buf.reshape((peers, capacity) + send_buf.shape[1:])
        recvs = [send_buf[0]] + [lax.ppermute(send_buf[step], "skyx", rings[step]) for step in range(1, peers)]
        upper, lower, interior = place(recv_rows, recvs, after, positions, margin, inner)
        from_above = shifted(lower, "skyy", 1)
        from_below = shifted(upper, "skyy", -1)
        from_above = from_above.astype(jnp.float32)
        from_below = from_below.astype(jnp.float32)
        after = [upper]
        interior = interior.at[:margin].add(from_above)
        interior = interior.at[inner - margin :].add(from_below)
        interiors.append(interior)

    left_part = interiors[0][..., :tile_width].astype(jnp.bfloat16)
    width = interiors[-1].shape[-1]
    right_part = interiors[-1][..., width - tile_width :].astype(jnp.bfloat16)
    from_left = shifted(right_part, "skyx", 1).astype(jnp.float32)
    from_right = shifted(left_part, "skyx", -1).astype(jnp.float32)
    first = interiors[0][..., tile_width:]
    first = first.at[..., :tile_width].add(from_left)
    last = interiors[-1][..., : width - tile_width]
    last = last.at[..., width - 2 * tile_width :].add(from_right)
    core = jnp.concatenate([first] + interiors[1:-1] + [last], axis=-1)
    num = core[:, 0].reshape(PR, pw)
    den = core[:, 1].reshape(PR, pw)
    return num / jnp.maximum(den, 1.0)


def solution(mesh):
    in_specs = (
        P(("tract", "skyy"), "skyx", None, None),
        P(("tract", "skyy"), "skyx", None, None),
        P(("tract", "skyy"), "skyx", None, None),
        P("tract", None, None),
        P(("tract", "skyy"), None),
        P(("tract", "skyy"), "skyx", None),
        P(("tract", "skyy"), "skyx"),
    )
    out_specs = P(("tract", "skyy"), "skyx")
    return jax.shard_map(local_body, mesh=mesh, in_specs=in_specs, out_specs=out_specs, check_vma=False)
```

profile of v0, /device:TPU:1, one launch (start us, length us, event | category | flops | bytes accessed | tf_op | source)
XLA Modules:
  0.0 134.3 jit_solution(14423597012917705193)
XLA Ops:
  1.5 5.9 %all-gather.1 = s32[4,2,32]{2,1,0:T(2,128)S(1)} all-gather(s32[1,2,32]{2,1,0:T(2,128)S(1)} %add_bitcast_fusion), channel_id=2, replica_groups=mesh['tract'=2,'skyx'=4,'skyy'=4] {'skyx'}, dimensions={0}, use_global_device_ids=true | all-gather | bytes 1280 | tf_op jit(solution)/shard_map/all_gather | solution.py:186
  9.8 1.7 %copy-done.1 = bf16[1,2,136,4480]{3,2,1,0:T(8,128)(2,1)S(1)} copy-done((bf16[1,2,136,4480]{3,2,1,0:T(8,128)(2,1)S(1)}, bf16[1,2,136,4480]{3,2,1,0:T(8,128)(2,1)}, u32[]{:S(2)}) %copy-start.1) | copy-done | bytes 2437144
  11.5 4.8 %shard_map.73.prev_ref = bf16[48,2,8,640]{3,2,1,0:T(8,128)(2,1)S(1)} custom-call(f32[2]{0:T(128)S(1)} %fusion.16.w_ref, s32[48]{0:T(128)S(1)} %min.12.idx_ref, bf16[1,2,136,4480]{3,2,1,0:T(8,128)(2,1)S(1)} %copy-done.1, s32[1,2,136,4480]{3,2,1,0:T(8,128)} %mask_hbm.7, bf16[1,2,128,136]{3,2,1,0:T(8,128)(2,1)S(1)} %copy.22.rk_ref, ...), custom_call_target="tpu_custom_call" | custom-call | flops 501219328 | bytes 2936832 | tf_op jit(solution)/shard_map/pallas_call | solution.py:85
  16.6 1.7 %collective-permute-start.1 = (bf16[12,2,8,640]{3,2,1,0:T(8,128)(2,1)S(1)}, bf16[12,2,8,640]{3,2,1,0:T(8,128)(2,1)S(1)}, u32[]{:S(2)}, u32[]{:S(2)}) collective-permute-start(bf16[12,2,8,640]{3,2,1,0:T(8,128)(2,1)S(1)} %get-tuple-element.164), channel_id=1, source_target_pairs={{0,8},{4,12},{8,0},{12,4},{1,9},{5,13},{9,1},{13,5},{2,10},{6,14},... | collective-permute-start | bytes 737288 | tf_op jit(solution)/shard_map/ppermute | solution.py:206
  18.3 1.9 %collective-permute-start = (bf16[12,2,8,640]{3,2,1,0:T(8,128)(2,1)S(1)}, bf16[12,2,8,640]{3,2,1,0:T(8,128)(2,1)S(1)}, u32[]{:S(2)}, u32[]{:S(2)}) collective-permute-start(bf16[12,2,8,640]{3,2,1,0:T(8,128)(2,1)S(1)} %get-tuple-element.165), channel_id=1, source_target_pairs={{0,4},{4,8},{8,12},{12,0},{1,5},{5,9},{9,13},{13,1},{2,6},{6,10},{... | collective-permute-start | bytes 737288 | tf_op jit(solution)/shard_map/ppermute | solution.py:206
  20.2 7.9 %shard_map.75.prev_ref = bf16[48,2,8,1408]{3,2,1,0:T(8,128)(2,1)S(1)} custom-call(f32[2]{0:T(128)S(1)} %fusion.16.w_ref, s32[48]{0:T(128)S(1)} %min.12.idx_ref, bf16[1,2,136,4480]{3,2,1,0:T(8,128)(2,1)S(1)} %copy-done.1, s32[1,2,136,4480]{3,2,1,0:T(8,128)} %mask_hbm.7, bf16[1,2,128,136]{3,2,1,0:T(8,128)(2,1)S(1)} %copy.22.rk_ref, ...), custom_call_target="tpu_custom_call" | custom-call | flops 1017118720 | bytes 5959680 | tf_op jit(solution)/shard_map/pallas_call | solution.py:85
  28.4 8.0 %shard_map.76.prev_ref = bf16[48,2,8,1408]{3,2,1,0:T(8,128)(2,1)S(1)} custom-call(f32[2]{0:T(128)S(1)} %fusion.16.w_ref, s32[48]{0:T(128)S(1)} %min.12.idx_ref, bf16[1,2,136,4480]{3,2,1,0:T(8,128)(2,1)} %img_hbm.7, s32[1,2,136,4480]{3,2,1,0:T(8,128)} %mask_hbm.7, bf16[1,2,128,136]{3,2,1,0:T(8,128)(2,1)S(1)} %copy.22.rk_ref, bf16[33,384,128]{2,1,0:T(8,128)(2,1)} %ck_hbm.7, ...), custom_call_target="tpu_custom_call" | custom-call | flops 1017118720 | bytes 5959680 | tf_op jit(solution)/shard_map/pallas_call | solution.py:85
  36.4 1.8 %collective-permute-start.11 = (bf16[12,2,8,1408]{3,2,1,0:T(8,128)(2,1)S(1)}, bf16[12,2,8,1408]{3,2,1,0:T(8,128)(2,1)S(1)}, u32[]{:S(2)}, u32[]{:S(2)}) collective-permute-start(bf16[12,2,8,1408]{3,2,1,0:T(8,128)(2,1)S(1)} %get-tuple-element.153), channel_id=1, source_target_pairs={{0,4},{4,8},{8,12},{12,0},{1,5},{5,9},{9,13},{13,1},{2,6},{6,10},{... | collective-permute-start | bytes 1622024 | tf_op jit(solution)/shard_map/ppermute | solution.py:206
  39.7 3.7 %collective-permute-start.3 = (bf16[8,2,8,640]{3,2,1,0:T(8,128)(2,1)S(1)}, bf16[8,2,8,640]{3,2,1,0:T(8,128)(2,1)S(1)}, u32[]{:S(2)}, u32[]{:S(2)}) collective-permute-start(bf16[8,2,8,640]{3,2,1,0:T(8,128)(2,1)S(1)} %get-tuple-element.138), channel_id=1, source_target_pairs={{0,1},{1,2},{2,3},{4,5},{5,6},{6,7},{8,9},{9,10},{10,11},{12,13},{... | collective-permute-start | bytes 491528 | tf_op jit(solution)/shard_map/ppermute | solution.py:19
  44.0 3.0 %collective-permute-done.3 = bf16[8,2,8,640]{3,2,1,0:T(8,128)(2,1)S(1)} collective-permute-done((bf16[8,2,8,640]{3,2,1,0:T(8,128)(2,1)S(1)}, bf16[8,2,8,640]{3,2,1,0:T(8,128)(2,1)S(1)}, u32[]{:S(2)}, u32[]{:S(2)}) %collective-permute-start.3) | collective-permute-done | bytes 163872 | tf_op jit(solution)/shard_map/ppermute | solution.py:19
  48.1 5.3 %shard_map.77 = bf16[48,2,8,768]{3,2,1,0:T(8,128)(2,1)S(1)} custom-call(f32[2]{0:T(128)S(1)} %fusion.16.w_ref, s32[48]{0:T(128)S(1)} %min.12.idx_ref, bf16[1,2,136,4480]{3,2,1,0:T(8,128)(2,1)S(1)} %copy-done.2, s32[1,2,136,4480]{3,2,1,0:T(8,128)} %mask_hbm.7, bf16[1,2,128,136]{3,2,1,0:T(8,128)(2,1)S(1)} %copy.22.rk_ref, bf16[33,384,128]{2,1,0:T(8,128)(2,1)} %ck_hbm.7, ...), custom_call_target="tpu_custom_call" | custom-call | flops 587202560 | bytes 3440640 | tf_op jit(solution)/shard_map/pallas_call | solution.py:85
  55.5 10.8 %collective-permute-done.10.refs_3_ = bf16[12,2,8,1408]{3,2,1,0:T(8,128)(2,1)S(1)} collective-permute-done((bf16[12,2,8,1408]{3,2,1,0:T(8,128)(2,1)S(1)}, bf16[12,2,8,1408]{3,2,1,0:T(8,128)(2,1)S(1)}, u32[]{:S(2)}, u32[]{:S(2)}) %collective-permute-start.10) | collective-permute-done | bytes 540704 | tf_op jit(solution)/shard_map/ppermute | solution.py:206
  67.7 1.7 %shard_map.78 = (bf16[8,2,8,1408]{3,2,1,0:T(8,128)(2,1)S(1)}, bf16[8,2,8,1408]{3,2,1,0:T(8,128)(2,1)S(1)}, f32[16,2,8,1408]{3,2,1,0:T(8,128)S(1)}) custom-call(s32[48]{0:T(128)S(1)} %sub.38.prev_ref.rows_ref.refs_4_, bf16[12,2,8,1408]{3,2,1,0:T(8,128)(2,1)S(1)} %get-tuple-element.154.refs_0_, bf16[12,2,8,1408]{3,2,1,0:T(8,128)(2,1)S(1)} %collective-permute-done.11.refs_1_, ...), custom_call_target="tpu_custom_call" | custom-call | tf_op jit(solution)/shard_map/pallas_call | solution.py:143
  69.4 5.9 %collective-permute-done.8.refs_1_ = bf16[12,2,8,1408]{3,2,1,0:T(8,128)(2,1)S(1)} collective-permute-done((bf16[12,2,8,1408]{3,2,1,0:T(8,128)(2,1)S(1)}, bf16[12,2,8,1408]{3,2,1,0:T(8,128)(2,1)S(1)}, u32[]{:S(2)}, u32[]{:S(2)}) %collective-permute-start.8) | collective-permute-done | bytes 540704 | tf_op jit(solution)/shard_map/ppermute | solution.py:206
  75.3 1.7 %shard_map.79 = (bf16[8,2,8,1408]{3,2,1,0:T(8,128)(2,1)S(1)}, bf16[8,2,8,1408]{3,2,1,0:T(8,128)(2,1)S(1)}, f32[16,2,8,1408]{3,2,1,0:T(8,128)S(1)}) custom-call(s32[48]{0:T(128)S(1)} %sub.38.prev_ref.rows_ref.refs_4_, bf16[12,2,8,1408]{3,2,1,0:T(8,128)(2,1)S(1)} %get-tuple-element.158.refs_0_, bf16[12,2,8,1408]{3,2,1,0:T(8,128)(2,1)S(1)} %collective-permute-done.8.refs_1_, ...), custom_call_target="tpu_custom_call" | custom-call | tf_op jit(solution)/shard_map/pallas_call | solution.py:143
  77.0 7.2 %collective-permute-done.7.refs_3_ = bf16[12,2,8,768]{3,2,1,0:T(8,128)(2,1)S(1)} collective-permute-done((bf16[12,2,8,768]{3,2,1,0:T(8,128)(2,1)S(1)}, bf16[12,2,8,768]{3,2,1,0:T(8,128)(2,1)S(1)}, u32[]{:S(2)}, u32[]{:S(2)}) %collective-permute-start.7) | collective-permute-done | bytes 294944 | tf_op jit(solution)/shard_map/ppermute | solution.py:206
  84.2 3.7 %collective-permute-done.5.refs_1_ = bf16[12,2,8,768]{3,2,1,0:T(8,128)(2,1)S(1)} collective-permute-done((bf16[12,2,8,768]{3,2,1,0:T(8,128)(2,1)S(1)}, bf16[12,2,8,768]{3,2,1,0:T(8,128)(2,1)S(1)}, u32[]{:S(2)}, u32[]{:S(2)}) %collective-permute-start.5) | collective-permute-done | bytes 294944 | tf_op jit(solution)/shard_map/ppermute | solution.py:206
  89.5 3.4 %collective-permute-start.14 = (bf16[8,2,8,768]{3,2,1,0:T(8,128)(2,1)S(1)}, bf16[8,2,8,768]{3,2,1,0:T(8,128)(2,1)S(1)}, u32[]{:S(2)}, u32[]{:S(2)}) collective-permute-start(bf16[8,2,8,768]{3,2,1,0:T(8,128)(2,1)S(1)} %get-tuple-element.143), channel_id=1, source_target_pairs={{0,1},{1,2},{2,3},{4,5},{5,6},{6,7},{8,9},{9,10},{10,11},{12,13},{... | collective-permute-start | bytes 589832 | tf_op jit(solution)/shard_map/ppermute | solution.py:19
  93.0 4.7 %collective-permute-start.21 = (bf16[16,2,8,128]{3,2,1,0:T(8,128)(2,1)S(1)}, bf16[16,2,8,128]{3,2,1,0:T(8,128)(2,1)S(1)}, u32[]{:S(2)}, u32[]{:S(2)}) collective-permute-start(bf16[16,2,8,128]{3,2,1,0:T(8,128)(2,1)S(1)} %slice.478), channel_id=1, source_target_pairs={{4,0},{8,4},{12,8},{5,1},{9,5},{13,9},{6,2},{10,6},{14,10},{7,3},{... | collective-permute-start | bytes 196616 | tf_op jit(solution)/shard_map/ppermute | solution.py:19
  100.3 4.6 %collective-permute-start.17 = (bf16[8,2,8,1408]{3,2,1,0:T(8,128)(2,1)S(1)}, bf16[8,2,8,1408]{3,2,1,0:T(8,128)(2,1)S(1)}, u32[]{:S(2)}, u32[]{:S(2)}) collective-permute-start(bf16[8,2,8,1408]{3,2,1,0:T(8,128)(2,1)S(1)} %get-tuple-element.146), channel_id=1, source_target_pairs={{0,1},{1,2},{2,3},{4,5},{5,6},{6,7},{8,9},{9,10},{10,11},{12,13},{... | collective-permute-start | bytes 1081352 | tf_op jit(solution)/shard_map/ppermute | solution.py:19
  106.3 15.3 %collective-permute-done.15 = bf16[8,2,8,768]{3,2,1,0:T(8,128)(2,1)S(1)} collective-permute-done((bf16[8,2,8,768]{3,2,1,0:T(8,128)(2,1)S(1)}, bf16[8,2,8,768]{3,2,1,0:T(8,128)(2,1)S(1)}, u32[]{:S(2)}, u32[]{:S(2)}) %collective-permute-start.15) | collective-permute-done | bytes 196640 | tf_op jit(solution)/shard_map/ppermute | solution.py:19
  121.6 3.2 %collective-permute-start.19 = (bf16[8,2,8,1408]{3,2,1,0:T(8,128)(2,1)S(1)}, bf16[8,2,8,1408]{3,2,1,0:T(8,128)(2,1)S(1)}, u32[]{:S(2)}, u32[]{:S(2)}) collective-permute-start(bf16[8,2,8,1408]{3,2,1,0:T(8,128)(2,1)S(1)} %get-tuple-element.148), channel_id=1, source_target_pairs={{0,1},{1,2},{2,3},{4,5},{5,6},{6,7},{8,9},{9,10},{10,11},{12,13},{... | collective-permute-start | bytes 1081352 | tf_op jit(solution)/shard_map/ppermute | solution.py:19
  125.0 3.2 %collective-permute-start.16 = (bf16[16,2,8,128]{3,2,1,0:T(8,128)(2,1)S(1)}, bf16[16,2,8,128]{3,2,1,0:T(8,128)(2,1)S(1)}, u32[]{:S(2)}, u32[]{:S(2)}) collective-permute-start(bf16[16,2,8,128]{3,2,1,0:T(8,128)(2,1)S(1)} %slice.479), channel_id=1, source_target_pairs={{0,4},{4,8},{8,12},{1,5},{5,9},{9,13},{2,6},{6,10},{10,14},{3,7},{... | collective-permute-start | bytes 196616 | tf_op jit(solution)/shard_map/ppermute | solution.py:19
  129.8 2.3 %collective-permute-done.19 = bf16[8,2,8,1408]{3,2,1,0:T(8,128)(2,1)S(1)} collective-permute-done((bf16[8,2,8,1408]{3,2,1,0:T(8,128)(2,1)S(1)}, bf16[8,2,8,1408]{3,2,1,0:T(8,128)(2,1)S(1)}, u32[]{:S(2)}, u32[]{:S(2)}) %collective-permute-start.19) | collective-permute-done | bytes 360480 | tf_op jit(solution)/shard_map/ppermute | solution.py:19
  (78 shorter events, 20.5 us)
Async XLA Ops:
  0.0 9.7 %copy-start = (f32[1,8]{1,0:T(1,128)S(1)}, f32[1,8]{1,0:T(1,128)}, u32[]{:S(2)}) copy-start(f32[1,8]{1,0:T(1,128)} %param.31) | copy-start | bytes 100
  16.4 20.0 %collective-permute-start.2 = (bf16[12,2,8,640]{3,2,1,0:T(8,128)(2,1)S(1)}, bf16[12,2,8,640]{3,2,1,0:T(8,128)(2,1)S(1)}, u32[]{:S(2)}, u32[]{:S(2)}) collective-permute-start(bf16[12,2,8,640]{3,2,1,0:T(8,128)(2,1)S(1)} %get-tuple-element.163), channel_id=1, source_target_pairs={{0,12},{4,0},{8,4},{12,8},{1,13},{5,1},{9,5},{13,9},{2,14},{6,2},{... | collective-permute-start | bytes 737288 | tf_op jit(solution)/shard_map/ppermute | solution.py:206
  16.6 21.6 %collective-permute-start.1 = (bf16[12,2,8,640]{3,2,1,0:T(8,128)(2,1)S(1)}, bf16[12,2,8,640]{3,2,1,0:T(8,128)(2,1)S(1)}, u32[]{:S(2)}, u32[]{:S(2)}) collective-permute-start(bf16[12,2,8,640]{3,2,1,0:T(8,128)(2,1)S(1)} %get-tuple-element.164), channel_id=1, source_target_pairs={{0,8},{4,12},{8,0},{12,4},{1,9},{5,13},{9,1},{13,5},{2,10},{6,14},... | collective-permute-start | bytes 737288 | tf_op jit(solution)/shard_map/ppermute | solution.py:206
  18.3 19.9 %collective-permute-start = (bf16[12,2,8,640]{3,2,1,0:T(8,128)(2,1)S(1)}, bf16[12,2,8,640]{3,2,1,0:T(8,128)(2,1)S(1)}, u32[]{:S(2)}, u32[]{:S(2)}) collective-permute-start(bf16[12,2,8,640]{3,2,1,0:T(8,128)(2,1)S(1)} %get-tuple-element.165), channel_id=1, source_target_pairs={{0,4},{4,8},{8,12},{12,0},{1,5},{5,9},{9,13},{13,1},{2,6},{6,10},{... | collective-permute-start | bytes 737288 | tf_op jit(solution)/shard_map/ppermute | solution.py:206
  28.2 25.2 %collective-permute-start.13 = (bf16[12,2,8,1408]{3,2,1,0:T(8,128)(2,1)S(1)}, bf16[12,2,8,1408]{3,2,1,0:T(8,128)(2,1)S(1)}, u32[]{:S(2)}, u32[]{:S(2)}) collective-permute-start(bf16[12,2,8,1408]{3,2,1,0:T(8,128)(2,1)S(1)} %get-tuple-element.151), channel_id=1, source_target_pairs={{0,12},{4,0},{8,4},{12,8},{1,13},{5,1},{9,5},{13,9},{2,14},{6,2},{... | collective-permute-start | bytes 1622024 | tf_op jit(solution)/shard_map/ppermute | solution.py:206
  28.3 26.7 %collective-permute-start.12 = (bf16[12,2,8,1408]{3,2,1,0:T(8,128)(2,1)S(1)}, bf16[12,2,8,1408]{3,2,1,0:T(8,128)(2,1)S(1)}, u32[]{:S(2)}, u32[]{:S(2)}) collective-permute-start(bf16[12,2,8,1408]{3,2,1,0:T(8,128)(2,1)S(1)} %get-tuple-element.152), channel_id=1, source_target_pairs={{0,8},{4,12},{8,0},{12,4},{1,9},{5,13},{9,1},{13,5},{2,10},{6,14},... | collective-permute-start | bytes 1622024 | tf_op jit(solution)/shard_map/ppermute | solution.py:206
  36.4 18.7 %collective-permute-start.11 = (bf16[12,2,8,1408]{3,2,1,0:T(8,128)(2,1)S(1)}, bf16[12,2,8,1408]{3,2,1,0:T(8,128)(2,1)S(1)}, u32[]{:S(2)}, u32[]{:S(2)}) collective-permute-start(bf16[12,2,8,1408]{3,2,1,0:T(8,128)(2,1)S(1)} %get-tuple-element.153), channel_id=1, source_target_pairs={{0,4},{4,8},{8,12},{12,0},{1,5},{5,9},{9,13},{13,1},{2,6},{6,10},{... | collective-permute-start | bytes 1622024 | tf_op jit(solution)/shard_map/ppermute | solution.py:206
  39.7 8.4 %copy-start.2 = (bf16[1,2,136,4480]{3,2,1,0:T(8,128)(2,1)S(1)}, bf16[1,2,136,4480]{3,2,1,0:T(8,128)(2,1)}, u32[]{:S(2)}) copy-start(bf16[1,2,136,4480]{3,2,1,0:T(8,128)(2,1)} %img_hbm.7) | copy-start | bytes 7311364
  39.7 7.2 %collective-permute-start.3 = (bf16[8,2,8,640]{3,2,1,0:T(8,128)(2,1)S(1)}, bf16[8,2,8,640]{3,2,1,0:T(8,128)(2,1)S(1)}, u32[]{:S(2)}, u32[]{:S(2)}) collective-permute-start(bf16[8,2,8,640]{3,2,1,0:T(8,128)(2,1)S(1)} %get-tuple-element.138), channel_id=1, source_target_pairs={{0,1},{1,2},{2,3},{4,5},{5,6},{6,7},{8,9},{9,10},{10,11},{12,13},{... | collective-permute-start | bytes 491528 | tf_op jit(solution)/shard_map/ppermute | solution.py:19
  43.6 22.7 %collective-permute-start.10 = (bf16[12,2,8,1408]{3,2,1,0:T(8,128)(2,1)S(1)}, bf16[12,2,8,1408]{3,2,1,0:T(8,128)(2,1)S(1)}, u32[]{:S(2)}, u32[]{:S(2)}) collective-permute-start(bf16[12,2,8,1408]{3,2,1,0:T(8,128)(2,1)S(1)} %get-tuple-element.155), channel_id=1, source_target_pairs={{0,12},{4,0},{8,4},{12,8},{1,13},{5,1},{9,5},{13,9},{2,14},{6,2},{... | collective-permute-start | bytes 1622024 | tf_op jit(solution)/shard_map/ppermute | solution.py:206
  47.0 19.4 %collective-permute-start.9 = (bf16[12,2,8,1408]{3,2,1,0:T(8,128)(2,1)S(1)}, bf16[12,2,8,1408]{3,2,1,0:T(8,128)(2,1)S(1)}, u32[]{:S(2)}, u32[]{:S(2)}) collective-permute-start(bf16[12,2,8,1408]{3,2,1,0:T(8,128)(2,1)S(1)} %get-tuple-element.156), channel_id=1, source_target_pairs={{0,8},{4,12},{8,0},{12,4},{1,9},{5,13},{9,1},{13,5},{2,10},{6,14},... | collective-permute-start | bytes 1622024 | tf_op jit(solution)/shard_map/ppermute | solution.py:206
  53.4 21.9 %collective-permute-start.8 = (bf16[12,2,8,1408]{3,2,1,0:T(8,128)(2,1)S(1)}, bf16[12,2,8,1408]{3,2,1,0:T(8,128)(2,1)S(1)}, u32[]{:S(2)}, u32[]{:S(2)}) collective-permute-start(bf16[12,2,8,1408]{3,2,1,0:T(8,128)(2,1)S(1)} %get-tuple-element.157), channel_id=1, source_target_pairs={{0,4},{4,8},{8,12},{12,0},{1,5},{5,9},{9,13},{13,1},{2,6},{6,10},{... | collective-permute-start | bytes 1622024 | tf_op jit(solution)/shard_map/ppermute | solution.py:206
  55.0 29.3 %collective-permute-start.7 = (bf16[12,2,8,768]{3,2,1,0:T(8,128)(2,1)S(1)}, bf16[12,2,8,768]{3,2,1,0:T(8,128)(2,1)S(1)}, u32[]{:S(2)}, u32[]{:S(2)}) collective-permute-start(bf16[12,2,8,768]{3,2,1,0:T(8,128)(2,1)S(1)} %get-tuple-element.159), channel_id=1, source_target_pairs={{0,12},{4,0},{8,4},{12,8},{1,13},{5,1},{9,5},{13,9},{2,14},{6,2},{... | collective-permute-start | bytes 884744 | tf_op jit(solution)/shard_map/ppermute | solution.py:206
  55.1 29.1 %collective-permute-start.6 = (bf16[12,2,8,768]{3,2,1,0:T(8,128)(2,1)S(1)}, bf16[12,2,8,768]{3,2,1,0:T(8,128)(2,1)S(1)}, u32[]{:S(2)}, u32[]{:S(2)}) collective-permute-start(bf16[12,2,8,768]{3,2,1,0:T(8,128)(2,1)S(1)} %get-tuple-element.160), channel_id=1, source_target_pairs={{0,8},{4,12},{8,0},{12,4},{1,9},{5,13},{9,1},{13,5},{2,10},{6,14},... | collective-permute-start | bytes 884744 | tf_op jit(solution)/shard_map/ppermute | solution.py:206
  66.3 21.6 %collective-permute-start.5 = (bf16[12,2,8,768]{3,2,1,0:T(8,128)(2,1)S(1)}, bf16[12,2,8,768]{3,2,1,0:T(8,128)(2,1)S(1)}, u32[]{:S(2)}, u32[]{:S(2)}) collective-permute-start(bf16[12,2,8,768]{3,2,1,0:T(8,128)(2,1)S(1)} %get-tuple-element.161), channel_id=1, source_target_pairs={{0,4},{4,8},{8,12},{12,0},{1,5},{5,9},{9,13},{13,1},{2,6},{6,10},{... | collective-permute-start | bytes 884744 | tf_op jit(solution)/shard_map/ppermute | solution.py:206
  66.3 26.5 %collective-permute-start.4 = (bf16[8,2,8,640]{3,2,1,0:T(8,128)(2,1)S(1)}, bf16[8,2,8,640]{3,2,1,0:T(8,128)(2,1)S(1)}, u32[]{:S(2)}, u32[]{:S(2)}) collective-permute-start(bf16[8,2,8,640]{3,2,1,0:T(8,128)(2,1)S(1)} %get-tuple-element.139.refs_4_), channel_id=1, source_target_pairs={{1,0},{2,1},{3,2},{5,4},{6,5},{7,6},{9,8},{10,9},{11,10},{13,12},{... | collective-permute-start | bytes 491528 | tf_op jit(solution)/shard_map/ppermute | solution.py:19
  89.5 15.5 %collective-permute-start.14 = (bf16[8,2,8,768]{3,2,1,0:T(8,128)(2,1)S(1)}, bf16[8,2,8,768]{3,2,1,0:T(8,128)(2,1)S(1)}, u32[]{:S(2)}, u32[]{:S(2)}) collective-permute-start(bf16[8,2,8,768]{3,2,1,0:T(8,128)(2,1)S(1)} %get-tuple-element.143), channel_id=1, source_target_pairs={{0,1},{1,2},{2,3},{4,5},{5,6},{6,7},{8,9},{9,10},{10,11},{12,13},{... | collective-permute-start | bytes 589832 | tf_op jit(solution)/shard_map/ppermute | solution.py:19
  93.0 32.0 %collective-permute-start.21 = (bf16[16,2,8,128]{3,2,1,0:T(8,128)(2,1)S(1)}, bf16[16,2,8,128]{3,2,1,0:T(8,128)(2,1)S(1)}, u32[]{:S(2)}, u32[]{:S(2)}) collective-permute-start(bf16[16,2,8,128]{3,2,1,0:T(8,128)(2,1)S(1)} %slice.478), channel_id=1, source_target_pairs={{4,0},{8,4},{12,8},{5,1},{9,5},{13,9},{6,2},{10,6},{14,10},{7,3},{... | collective-permute-start | bytes 196616 | tf_op jit(solution)/shard_map/ppermute | solution.py:19
  97.7 32.0 %collective-permute-start.18 = (bf16[8,2,8,1408]{3,2,1,0:T(8,128)(2,1)S(1)}, bf16[8,2,8,1408]{3,2,1,0:T(8,128)(2,1)S(1)}, u32[]{:S(2)}, u32[]{:S(2)}) collective-permute-start(bf16[8,2,8,1408]{3,2,1,0:T(8,128)(2,1)S(1)} %get-tuple-element.140.refs_4_), channel_id=1, source_target_pairs={{1,0},{2,1},{3,2},{5,4},{6,5},{7,6},{9,8},{10,9},{11,10},{13,12},{... | collective-permute-start | bytes 1081352 | tf_op jit(solution)/shard_map/ppermute | solution.py:19
  99.0 33.3 %collective-permute-start.20 = (bf16[8,2,8,1408]{3,2,1,0:T(8,128)(2,1)S(1)}, bf16[8,2,8,1408]{3,2,1,0:T(8,128)(2,1)S(1)}, u32[]{:S(2)}, u32[]{:S(2)}) collective-permute-start(bf16[8,2,8,1408]{3,2,1,0:T(8,128)(2,1)S(1)} %get-tuple-element.141.refs_4_), channel_id=1, source_target_pairs={{1,0},{2,1},{3,2},{5,4},{6,5},{7,6},{9,8},{10,9},{11,10},{13,12},{... | collective-permute-start | bytes 1081352 | tf_op jit(solution)/shard_map/ppermute | solution.py:19
  100.3 29.3 %collective-permute-start.17 = (bf16[8,2,8,1408]{3,2,1,0:T(8,128)(2,1)S(1)}, bf16[8,2,8,1408]{3,2,1,0:T(8,128)(2,1)S(1)}, u32[]{:S(2)}, u32[]{:S(2)}) collective-permute-start(bf16[8,2,8,1408]{3,2,1,0:T(8,128)(2,1)S(1)} %get-tuple-element.146), channel_id=1, source_target_pairs={{0,1},{1,2},{2,3},{4,5},{5,6},{6,7},{8,9},{9,10},{10,11},{12,13},{... | collective-permute-start | bytes 1081352 | tf_op jit(solution)/shard_map/ppermute | solution.py:19
  104.9 16.7 %collective-permute-start.15 = (bf16[8,2,8,768]{3,2,1,0:T(8,128)(2,1)S(1)}, bf16[8,2,8,768]{3,2,1,0:T(8,128)(2,1)S(1)}, u32[]{:S(2)}, u32[]{:S(2)}) collective-permute-start(bf16[8,2,8,768]{3,2,1,0:T(8,128)(2,1)S(1)} %get-tuple-element.144), channel_id=1, source_target_pairs={{1,0},{2,1},{3,2},{5,4},{6,5},{7,6},{9,8},{10,9},{11,10},{13,12},{... | collective-permute-start | bytes 589832 | tf_op jit(solution)/shard_map/ppermute | solution.py:19
  121.6 10.6 %collective-permute-start.19 = (bf16[8,2,8,1408]{3,2,1,0:T(8,128)(2,1)S(1)}, bf16[8,2,8,1408]{3,2,1,0:T(8,128)(2,1)S(1)}, u32[]{:S(2)}, u32[]{:S(2)}) collective-permute-start(bf16[8,2,8,1408]{3,2,1,0:T(8,128)(2,1)S(1)} %get-tuple-element.148), channel_id=1, source_target_pairs={{0,1},{1,2},{2,3},{4,5},{5,6},{6,7},{8,9},{9,10},{10,11},{12,13},{... | collective-permute-start | bytes 1081352 | tf_op jit(solution)/shard_map/ppermute | solution.py:19
  125.0 4.5 %collective-permute-start.16 = (bf16[16,2,8,128]{3,2,1,0:T(8,128)(2,1)S(1)}, bf16[16,2,8,128]{3,2,1,0:T(8,128)(2,1)S(1)}, u32[]{:S(2)}, u32[]{:S(2)}) collective-permute-start(bf16[16,2,8,128]{3,2,1,0:T(8,128)(2,1)S(1)} %slice.479), channel_id=1, source_target_pairs={{0,4},{4,8},{8,12},{1,5},{5,9},{9,13},{2,6},{6,10},{10,14},{3,7},{... | collective-permute-start | bytes 196616 | tf_op jit(solution)/shard_map/ppermute | solution.py:19
  (1 other events, 1.7 us)
where the time goes:
time: 136 us; the launch traced here: 134 us
  waiting for transfers between devices  49.5 us (36%)
  starting transfers between devices  37.2 us (27%)
  Pallas kernels  32.3 us (24%)
  blocking collectives  5.88 us (4%)
  other arithmetic  4.81 us (4%)
  local copies, waits for them, and re-layouts  3.79 us (3%)
    ppermute x10, starting transfers between devices, shifted(): lax.ppermute(value, axis, [(source, source + steps) for source in range(f...  28 us
    ppermute x12, waiting for transfers between devices, local_body(): lax.ppermute(send_buf[step], 'skyx', rings[step])  27.6 us
    pallas_call x4, Pallas kernels, warp_chunk(): pl.pallas_call(make_warp_kernel(start, window, first_tile, exposures), in...  25.9 us
    ppermute x10, waiting for transfers between devices, shifted(): lax.ppermute(value, axis, [(source, source + steps) for source in range(f...  21.9 us
    ppermute x12, starting transfers between devices, local_body(): lax.ppermute(send_buf[step], 'skyx', rings[step])  9.27 us
    pallas_call x4, Pallas kernels, place(): pl.pallas_call(make_place_kernel(groups, capacity, positions, margin, inn...  6.4 us
    all_gather x1, blocking collectives, local_body(): table = lax.all_gather(jnp.stack([slot_dest, slot_rows]), 'skyx')  5.88 us
    unnamed x9, local copies, waits for them, and re-layouts  2.81 us
  transfers between devices with their start and end apart: 22, of which 8 were waited for; matrix products, arithmetic and copies ran while one was open for 1% of the time, Pallas kernels for 21%

commit v1 on v0

--- a/solution.py
+++ b/solution.py
@@ -9,7 +9,8 @@
 OVY = 64
 PR = 128
 RB = 8
-SPLIT = (5, 11, 11, 6)
+SPLIT = (5, 14, 6, 8)
+ORDER = (0, 3, 1, 2)
 ROW_PIECE = 640
 
 
@@ -195,10 +196,10 @@
 
     margin = OVY // RB
     inner = PR // RB
-    interiors = []
+    interiors = {}
     after = [recv_rows]
-    previous = recv_rows
-    for chunk in range(len(SPLIT)):
+    previous = send_idx
+    for chunk in ORDER:
         per = bounds[chunk + 1] - bounds[chunk]
         send_buf = warp_chunk(bounds[chunk], per, weights, send_idx, images, masks, row_kernels, col_kernel, previous)
         previous = send_buf
@@ -212,18 +213,21 @@
         after = [upper]
         interior = interior.at[:margin].add(from_above)
         interior = interior.at[inner - margin :].add(from_below)
-        interiors.append(interior)
-
-    left_part = interiors[0][..., :tile_width].astype(jnp.bfloat16)
-    width = interiors[-1].shape[-1]
-    right_part = interiors[-1][..., width - tile_width :].astype(jnp.bfloat16)
-    from_left = shifted(right_part, "skyx", 1).astype(jnp.float32)
-    from_right = shifted(left_part, "skyx", -1).astype(jnp.float32)
-    first = interiors[0][..., tile_width:]
+        interiors[chunk] = interior
+
+    left_edge = interiors[0]
+    right_edge = interiors[len(SPLIT) - 1]
+    width = right_edge.shape[-1]
+    from_left = shifted(right_edge[..., width - tile_width :].astype(jnp.bfloat16), "skyx", 1)
+    from_right = shifted(left_edge[..., :tile_width].astype(jnp.bfloat16), "skyx", -1)
+    from_left = from_left.astype(jnp.float32)
+    from_right = from_right.astype(jnp.float32)
+    first = left_edge[..., tile_width:]
     first = first.at[..., :tile_width].add(from_left)
-    last = interiors[-1][..., : width - tile_width]
+    last = right_edge[..., : width - tile_width]
     last = last.at[..., width - 2 * tile_width :].add(from_right)
-    core = jnp.concatenate([first] + interiors[1:-1] + [last], axis=-1)
+    middle = [interiors[c] for c in range(1, len(SPLIT) - 1)]
+    core = jnp.concatenate([first] + middle + [last], axis=-1)
     num = core[:, 0].reshape(PR, pw)
     den = core[:, 1].reshape(PR, pw)
     return num / jnp.maximum(den, 1.0)

time: 136 us -> 128 us (0.941)
  the two profiles are of different devices: /device:TPU:1 before, /device:TPU:0 now
where the time goes in v1:
time: 128 us; the launch traced here: 127 us
  starting transfers between devices  39.5 us (31%)
  Pallas kernels  35.7 us (28%)
  waiting for transfers between devices  23.2 us (18%)
  blocking collectives  14.9 us (12%)
  local copies, waits for them, and re-layouts  8.7 us (7%)
  other arithmetic  4.26 us (3%)
    pallas_call x4, Pallas kernels, warp_chunk(): pl.pallas_call(make_warp_kernel(start, window, first_tile, exposures), in...  27.3 us
    ppermute x10, starting transfers between devices, shifted(): lax.ppermute(value, axis, [(source, source + steps) for source in range(f...  24.8 us
    all_gather x1, blocking collectives, local_body(): table = lax.all_gather(jnp.stack([slot_dest, slot_rows]), 'skyx')  14.9 us
    ppermute x12, starting transfers between devices, local_body(): lax.ppermute(send_buf[step], 'skyx', rings[step])  14.7 us
    ppermute x10, waiting for transfers between devices, shifted(): lax.ppermute(value, axis, [(source, source + steps) for source in range(f...  13.7 us
    ppermute x12, waiting for transfers between devices, local_body(): lax.ppermute(send_buf[step], 'skyx', rings[step])  9.5 us
    pallas_call x4, Pallas kernels, place(): pl.pallas_call(make_place_kernel(groups, capacity, positions, margin, inn...  8.41 us
    slice x4, local copies, waits for them, and re-layouts, local_body(): send_buf[step]  5.37 us
  transfers between devices with their start and end apart: 22, of which 9 were waited for; matrix products, arithmetic and copies ran while one was open for 5% of the time, Pallas kernels for 24%

profile of v1, /device:TPU:0, one launch (start us, length us, event | category | flops | bytes accessed | tf_op | source)
XLA Modules:
  0.0 127.1 jit_solution(10444349894844074316)
XLA Ops:
  2.4 1.7 %copy-done.1 = bf16[1,2,136,4480]{3,2,1,0:T(8,128)(2,1)S(1)} copy-done((bf16[1,2,136,4480]{3,2,1,0:T(8,128)(2,1)S(1)}, bf16[1,2,136,4480]{3,2,1,0:T(8,128)(2,1)}, u32[]{:S(2)}) %copy-start.1) | copy-done | bytes 2437144
  4.1 4.8 %shard_map.73.prev_ref = bf16[48,2,8,640]{3,2,1,0:T(8,128)(2,1)S(1)} custom-call(f32[2]{0:T(128)S(1)} %fusion.16.w_ref, s32[48]{0:T(128)S(1)} %min.12.idx_ref.prev_ref, bf16[1,2,136,4480]{3,2,1,0:T(8,128)(2,1)S(1)} %copy-done.1, s32[1,2,136,4480]{3,2,1,0:T(8,128)} %mask_hbm.7, bf16[1,2,128,136]{3,2,1,0:T(8,128)(2,1)S(1)} %copy.22.rk_ref, ...), custom_call_target="tpu_custom_call" | custom-call | flops 501219328 | bytes 2936832 | tf_op jit(solution)/shard_map/pallas_call | solution.py:86
  9.8 2.4 %collective-permute-start.2 = (bf16[12,2,8,640]{3,2,1,0:T(8,128)(2,1)}, bf16[12,2,8,640]{3,2,1,0:T(8,128)(2,1)}, u32[]{:S(2)}, u32[]{:S(2)}) collective-permute-start(bf16[12,2,8,640]{3,2,1,0:T(8,128)(2,1)} %get-tuple-element.163), channel_id=1, source_target_pairs={{0,12},{4,0},{8,4},{12,8},{1,13},{5,1},{9,5},{13,9},{2,14},{6,2},{... | collective-permute-start | bytes 737288 | tf_op jit(solution)/shard_map/ppermute | solution.py:207
  13.0 6.3 %shard_map.75.prev_ref = bf16[48,2,8,1024]{3,2,1,0:T(8,128)(2,1)S(1)} custom-call(f32[2]{0:T(128)S(1)} %fusion.16.w_ref, s32[48]{0:T(128)S(1)} %min.12.idx_ref.prev_ref, bf16[1,2,136,4480]{3,2,1,0:T(8,128)(2,1)S(1)} %copy-done.1, s32[1,2,136,4480]{3,2,1,0:T(8,128)} %mask_hbm.7, bf16[1,2,128,136]{3,2,1,0:T(8,128)(2,1)S(1)} %copy.22.rk_ref, ...), custom_call_target="tpu_custom_call" | custom-call | flops 759169024 | bytes 4448256 | tf_op jit(solution)/shard_map/pallas_call | solution.py:86
  23.5 14.9 %all-gather.1 = s32[4,2,32]{2,1,0:T(2,128)S(1)} all-gather(s32[1,2,32]{2,1,0:T(2,128)S(1)} %add_bitcast_fusion), channel_id=2, replica_groups=mesh['tract'=2,'skyx'=4,'skyy'=4] {'skyx'}, dimensions={0}, use_global_device_ids=true | all-gather | bytes 1280 | tf_op jit(solution)/shard_map/all_gather | solution.py:187
  38.5 10.9 %shard_map.77.prev_ref = bf16[48,2,8,1792]{3,2,1,0:T(8,128)(2,1)} custom-call(f32[2]{0:T(128)S(1)} %fusion.16.w_ref, s32[48]{0:T(128)S(1)} %min.12.idx_ref.prev_ref, bf16[1,2,136,4480]{3,2,1,0:T(8,128)(2,1)S(1)} %copy-done.1, s32[1,2,136,4480]{3,2,1,0:T(8,128)} %mask_hbm.7, bf16[1,2,128,136]{3,2,1,0:T(8,128)(2,1)S(1)} %copy.22.rk_ref, ...), custom_call_target="tpu_custom_call" | custom-call | flops 1275068416 | bytes 7471104 | tf_op jit(solution)/shard_map/pallas_call | solution.py:86
  49.9 3.2 %fusion.17 = (bf16[12,2,8,1792]{3,2,1,0:T(8,128)(2,1)}, bf16[12,2,8,1792]{3,2,1,0:T(8,128)(2,1)}, bf16[12,2,8,1792]{3,2,1,0:T(8,128)(2,1)}, bf16[12,2,8,1792]{3,2,1,0:T(8,128)(2,1)S(1)}) fusion(bf16[48,2,8,1792]{3,2,1,0:T(8,128)(2,1)} %shard_map.77.prev_ref), kind=kLoop, calls=%fused_computation.56 | loop fusion | bytes 5505024 | tf_op jit(solution)/shard_map/slice | solution.py:207
  53.8 5.3 %shard_map.79 = bf16[48,2,8,768]{3,2,1,0:T(8,128)(2,1)S(1)} custom-call(f32[2]{0:T(128)S(1)} %fusion.16.w_ref, s32[48]{0:T(128)S(1)} %min.12.idx_ref.prev_ref, bf16[1,2,136,4480]{3,2,1,0:T(8,128)(2,1)S(1)} %copy-done.2, s32[1,2,136,4480]{3,2,1,0:T(8,128)} %mask_hbm.7, bf16[1,2,128,136]{3,2,1,0:T(8,128)(2,1)S(1)} %copy.22.rk_ref, ...), custom_call_target="tpu_custom_call" | custom-call | flops 587202560 | bytes 3440640 | tf_op jit(solution)/shard_map/pallas_call | solution.py:86
  60.7 2.2 %shard_map.74 = (bf16[8,2,8,640]{3,2,1,0:T(8,128)(2,1)S(1)}, bf16[8,2,8,640]{3,2,1,0:T(8,128)(2,1)S(1)}, f32[16,2,8,640]{3,2,1,0:T(8,128)S(1)}) custom-call(s32[48]{0:T(128)S(1)} %sub.38.rows_ref.refs_4_, bf16[12,2,8,640]{3,2,1,0:T(8,128)(2,1)S(1)} %get-tuple-element.166.refs_0_, bf16[12,2,8,640]{3,2,1,0:T(8,128)(2,1)} %collective-permute-done.refs_1_, ...), custom_call_target="tpu_custom_call" | custom-call | tf_op jit(solution)/shard_map/pallas_call | solution.py:144
  62.9 3.7 %collective-permute-start.3 = (bf16[8,2,8,640]{3,2,1,0:T(8,128)(2,1)S(1)}, bf16[8,2,8,640]{3,2,1,0:T(8,128)(2,1)S(1)}, u32[]{:S(2)}, u32[]{:S(2)}) collective-permute-start(bf16[8,2,8,640]{3,2,1,0:T(8,128)(2,1)S(1)} %get-tuple-element.138), channel_id=1, source_target_pairs={{0,1},{1,2},{2,3},{4,5},{5,6},{6,7},{8,9},{9,10},{10,11},{12,13},{... | collective-permute-start | bytes 491528 | tf_op jit(solution)/shard_map/ppermute | solution.py:20
  69.5 2.4 %shard_map.76 = (bf16[8,2,8,1024]{3,2,1,0:T(8,128)(2,1)S(1)}, bf16[8,2,8,1024]{3,2,1,0:T(8,128)(2,1)S(1)}, f32[16,2,8,1024]{3,2,1,0:T(8,128)S(1)}) custom-call(s32[48]{0:T(128)S(1)} %sub.38.rows_ref.refs_4_, bf16[12,2,8,1024]{3,2,1,0:T(8,128)(2,1)S(1)} %copy-done.3, bf16[12,2,8,1024]{3,2,1,0:T(8,128)(2,1)} %collective-permute-done.5.refs_1_, ...), custom_call_target="tpu_custom_call" | custom-call | tf_op jit(solution)/shard_map/pallas_call | solution.py:144
  71.9 4.6 %collective-permute-start.8 = (bf16[8,2,8,1024]{3,2,1,0:T(8,128)(2,1)S(1)}, bf16[8,2,8,1024]{3,2,1,0:T(8,128)(2,1)S(1)}, u32[]{:S(2)}, u32[]{:S(2)}) collective-permute-start(bf16[8,2,8,1024]{3,2,1,0:T(8,128)(2,1)S(1)} %get-tuple-element.141), channel_id=1, source_target_pairs={{0,1},{1,2},{2,3},{4,5},{5,6},{6,7},{8,9},{9,10},{10,11},{12,13},{... | collective-permute-start | bytes 786440 | tf_op jit(solution)/shard_map/ppermute | solution.py:20
  78.3 4.2 %collective-permute-done.8 = bf16[8,2,8,1024]{3,2,1,0:T(8,128)(2,1)S(1)} collective-permute-done((bf16[8,2,8,1024]{3,2,1,0:T(8,128)(2,1)S(1)}, bf16[8,2,8,1024]{3,2,1,0:T(8,128)(2,1)S(1)}, u32[]{:S(2)}, u32[]{:S(2)}) %collective-permute-start.8) | collective-permute-done | bytes 262176 | tf_op jit(solution)/shard_map/ppermute | solution.py:20
  83.9 1.7 %collective-permute-done.21 = bf16[16,2,8,128]{3,2,1,0:T(8,128)(2,1)S(1)} collective-permute-done((bf16[16,2,8,128]{3,2,1,0:T(8,128)(2,1)S(1)}, bf16[16,2,8,128]{3,2,1,0:T(8,128)(2,1)S(1)}, u32[]{:S(2)}, u32[]{:S(2)}) %collective-permute-start.21) | collective-permute-done | bytes 65568 | tf_op jit(solution)/shard_map/ppermute | solution.py:20
  86.9 4.5 %collective-permute-start.17 = (bf16[12,2,8,768]{3,2,1,0:T(8,128)(2,1)S(1)}, bf16[12,2,8,768]{3,2,1,0:T(8,128)(2,1)S(1)}, u32[]{:S(2)}, u32[]{:S(2)}) collective-permute-start(bf16[12,2,8,768]{3,2,1,0:T(8,128)(2,1)S(1)} %get-tuple-element.160), channel_id=1, source_target_pairs={{0,8},{4,12},{8,0},{12,4},{1,9},{5,13},{9,1},{13,5},{2,10},{6,14},... | collective-permute-start | bytes 884744 | tf_op jit(solution)/shard_map/ppermute | solution.py:207
  91.6 2.1 %collective-permute-start.10 = (bf16[16,2,8,128]{3,2,1,0:T(8,128)(2,1)S(1)}, bf16[16,2,8,128]{3,2,1,0:T(8,128)(2,1)S(1)}, u32[]{:S(2)}, u32[]{:S(2)}) collective-permute-start(bf16[16,2,8,128]{3,2,1,0:T(8,128)(2,1)S(1)} %slice.479), channel_id=1, source_target_pairs={{0,4},{4,8},{8,12},{1,5},{5,9},{9,13},{2,6},{6,10},{10,14},{3,7},{... | collective-permute-start | bytes 196616 | tf_op jit(solution)/shard_map/ppermute | solution.py:20
  95.1 2.1 %shard_map.78 = (bf16[8,2,8,1792]{3,2,1,0:T(8,128)(2,1)S(1)}, bf16[8,2,8,1792]{3,2,1,0:T(8,128)(2,1)S(1)}, f32[16,2,8,1792]{3,2,1,0:T(8,128)S(1)}) custom-call(s32[48]{0:T(128)S(1)} %sub.38.rows_ref.refs_4_, bf16[12,2,8,1792]{3,2,1,0:T(8,128)(2,1)S(1)} %get-tuple-element.154.refs_0_, bf16[12,2,8,1792]{3,2,1,0:T(8,128)(2,1)S(1)} %collective-permute-done.11.refs_1_, ...), custom_call_target="tpu_custom_call" | custom-call | tf_op jit(solution)/shard_map/pallas_call | solution.py:144
  98.6 7.0 %collective-permute-done.17.refs_2_ = bf16[12,2,8,768]{3,2,1,0:T(8,128)(2,1)S(1)} collective-permute-done((bf16[12,2,8,768]{3,2,1,0:T(8,128)(2,1)S(1)}, bf16[12,2,8,768]{3,2,1,0:T(8,128)(2,1)S(1)}, u32[]{:S(2)}, u32[]{:S(2)}) %collective-permute-start.17) | collective-permute-done | bytes 294944 | tf_op jit(solution)/shard_map/ppermute | solution.py:207
  106.7 1.6 %shard_map.80 = (bf16[8,2,8,768]{3,2,1,0:T(8,128)(2,1)S(1)}, bf16[8,2,8,768]{3,2,1,0:T(8,128)(2,1)S(1)}, f32[16,2,8,768]{3,2,1,0:T(8,128)S(1)}) custom-call(s32[48]{0:T(128)S(1)} %sub.38.rows_ref.refs_4_, bf16[12,2,8,768]{3,2,1,0:T(8,128)(2,1)S(1)} %get-tuple-element.162.refs_0_, bf16[12,2,8,768]{3,2,1,0:T(8,128)(2,1)S(1)} %collective-permute-done.16.refs_1_, ...), custom_call_target="tpu_custom_call" | custom-call | tf_op jit(solution)/shard_map/pallas_call | solution.py:144
  108.3 3.5 %collective-permute-start.19 = (bf16[8,2,8,768]{3,2,1,0:T(8,128)(2,1)S(1)}, bf16[8,2,8,768]{3,2,1,0:T(8,128)(2,1)S(1)}, u32[]{:S(2)}, u32[]{:S(2)}) collective-permute-start(bf16[8,2,8,768]{3,2,1,0:T(8,128)(2,1)S(1)} %get-tuple-element.147), channel_id=1, source_target_pairs={{0,1},{1,2},{2,3},{4,5},{5,6},{6,7},{8,9},{9,10},{10,11},{12,13},{... | collective-permute-start | bytes 589832 | tf_op jit(solution)/shard_map/ppermute | solution.py:20
  113.1 4.6 %collective-permute-start.14 = (bf16[8,2,8,1792]{3,2,1,0:T(8,128)(2,1)S(1)}, bf16[8,2,8,1792]{3,2,1,0:T(8,128)(2,1)S(1)}, u32[]{:S(2)}, u32[]{:S(2)}) collective-permute-start(bf16[8,2,8,1792]{3,2,1,0:T(8,128)(2,1)S(1)} %get-tuple-element.144), channel_id=1, source_target_pairs={{0,1},{1,2},{2,3},{4,5},{5,6},{6,7},{8,9},{9,10},{10,11},{12,13},{... | collective-permute-start | bytes 1376264 | tf_op jit(solution)/shard_map/ppermute | solution.py:20
  117.8 1.5 %collective-permute-done.20 = bf16[8,2,8,768]{3,2,1,0:T(8,128)(2,1)S(1)} collective-permute-done((bf16[8,2,8,768]{3,2,1,0:T(8,128)(2,1)S(1)}, bf16[8,2,8,768]{3,2,1,0:T(8,128)(2,1)S(1)}, u32[]{:S(2)}, u32[]{:S(2)}) %collective-permute-start.20) | collective-permute-done | bytes 196640 | tf_op jit(solution)/shard_map/ppermute | solution.py:20
  119.5 5.3 %collective-permute-done.14 = bf16[8,2,8,1792]{3,2,1,0:T(8,128)(2,1)S(1)} collective-permute-done((bf16[8,2,8,1792]{3,2,1,0:T(8,128)(2,1)S(1)}, bf16[8,2,8,1792]{3,2,1,0:T(8,128)(2,1)S(1)}, u32[]{:S(2)}, u32[]{:S(2)}) %collective-permute-start.14) | collective-permute-done | bytes 458784 | tf_op jit(solution)/shard_map/ppermute | solution.py:20
  125.5 1.6 %fusion.1 = f32[128,3968]{1,0:T(8,128)} fusion(f32[16,2,8,3968]{3,2,1,0:T(8,128)S(1)} %pad_maximum_fusion), kind=kLoop, calls=%fused_computation.3 | loop fusion | flops 1015808 | bytes 6094848 | tf_op jit(solution)/shard_map/div | solution.py:233
  (90 shorter events, 24.4 us)
Async XLA Ops:
  9.8 43.6 %collective-permute-start.2 = (bf16[12,2,8,640]{3,2,1,0:T(8,128)(2,1)}, bf16[12,2,8,640]{3,2,1,0:T(8,128)(2,1)}, u32[]{:S(2)}, u32[]{:S(2)}) collective-permute-start(bf16[12,2,8,640]{3,2,1,0:T(8,128)(2,1)} %get-tuple-element.163), channel_id=1, source_target_pairs={{0,12},{4,0},{8,4},{12,8},{1,13},{5,1},{9,5},{13,9},{2,14},{6,2},{... | collective-permute-start | bytes 737288 | tf_op jit(solution)/shard_map/ppermute | solution.py:207
  12.2 47.0 %collective-permute-start.1 = (bf16[12,2,8,640]{3,2,1,0:T(8,128)(2,1)}, bf16[12,2,8,640]{3,2,1,0:T(8,128)(2,1)}, u32[]{:S(2)}, u32[]{:S(2)}) collective-permute-start(bf16[12,2,8,640]{3,2,1,0:T(8,128)(2,1)} %get-tuple-element.164), channel_id=1, source_target_pairs={{0,8},{4,12},{8,0},{12,4},{1,9},{5,13},{9,1},{13,5},{2,10},{6,14},... | collective-permute-start | bytes 737288 | tf_op jit(solution)/shard_map/ppermute | solution.py:207
  12.8 47.9 %collective-permute-start = (bf16[12,2,8,640]{3,2,1,0:T(8,128)(2,1)}, bf16[12,2,8,640]{3,2,1,0:T(8,128)(2,1)}, u32[]{:S(2)}, u32[]{:S(2)}) collective-permute-start(bf16[12,2,8,640]{3,2,1,0:T(8,128)(2,1)} %get-tuple-element.165), channel_id=1, source_target_pairs={{0,4},{4,8},{8,12},{12,0},{1,5},{5,9},{9,13},{13,1},{2,6},{6,10},{... | collective-permute-start | bytes 737288 | tf_op jit(solution)/shard_map/ppermute | solution.py:207
  20.5 46.2 %collective-permute-start.7 = (bf16[12,2,8,1024]{3,2,1,0:T(8,128)(2,1)}, bf16[12,2,8,1024]{3,2,1,0:T(8,128)(2,1)}, u32[]{:S(2)}, u32[]{:S(2)}) collective-permute-start(bf16[12,2,8,1024]{3,2,1,0:T(8,128)(2,1)} %get-tuple-element.155), channel_id=1, source_target_pairs={{0,12},{4,0},{8,4},{12,8},{1,13},{5,1},{9,5},{13,9},{2,14},{6,2},{... | collective-permute-start | bytes 1179656 | tf_op jit(solution)/shard_map/ppermute | solution.py:207
  22.0 46.1 %collective-permute-start.6 = (bf16[12,2,8,1024]{3,2,1,0:T(8,128)(2,1)}, bf16[12,2,8,1024]{3,2,1,0:T(8,128)(2,1)}, u32[]{:S(2)}, u32[]{:S(2)}) collective-permute-start(bf16[12,2,8,1024]{3,2,1,0:T(8,128)(2,1)} %get-tuple-element.156), channel_id=1, source_target_pairs={{0,8},{4,12},{8,0},{12,4},{1,9},{5,13},{9,1},{13,5},{2,10},{6,14},... | collective-permute-start | bytes 1179656 | tf_op jit(solution)/shard_map/ppermute | solution.py:207
  53.4 14.8 %collective-permute-start.5 = (bf16[12,2,8,1024]{3,2,1,0:T(8,128)(2,1)}, bf16[12,2,8,1024]{3,2,1,0:T(8,128)(2,1)}, u32[]{:S(2)}, u32[]{:S(2)}) collective-permute-start(bf16[12,2,8,1024]{3,2,1,0:T(8,128)(2,1)} %get-tuple-element.157), channel_id=1, source_target_pairs={{0,4},{4,8},{8,12},{12,0},{1,5},{5,9},{9,13},{13,1},{2,6},{6,10},{... | collective-permute-start | bytes 1179656 | tf_op jit(solution)/shard_map/ppermute | solution.py:207
  59.2 9.0 %copy-start.4 = (bf16[12,2,8,1792]{3,2,1,0:T(8,128)(2,1)S(1)}, bf16[12,2,8,1792]{3,2,1,0:T(8,128)(2,1)}, u32[]{:S(2)}) copy-start(bf16[12,2,8,1792]{3,2,1,0:T(8,128)(2,1)} %get-tuple-element.153) | copy-start | bytes 2064388
  59.2 10.3 %copy-start.3 = (bf16[12,2,8,1024]{3,2,1,0:T(8,128)(2,1)S(1)}, bf16[12,2,8,1024]{3,2,1,0:T(8,128)(2,1)}, u32[]{:S(2)}) copy-start(bf16[12,2,8,1024]{3,2,1,0:T(8,128)(2,1)} %get-tuple-element.158.refs_0_) | copy-start | bytes 1179652
  59.2 32.2 %collective-permute-start.13 = (bf16[12,2,8,1792]{3,2,1,0:T(8,128)(2,1)S(1)}, bf16[12,2,8,1792]{3,2,1,0:T(8,128)(2,1)S(1)}, u32[]{:S(2)}, u32[]{:S(2)}) collective-permute-start(bf16[12,2,8,1792]{3,2,1,0:T(8,128)(2,1)S(1)} %copy-done.6), channel_id=1, source_target_pairs={{0,12},{4,0},{8,4},{12,8},{1,13},{5,1},{9,5},{13,9},{2,14},{6,2},{... | collective-permute-start | bytes 2064392 | tf_op jit(solution)/shard_map/ppermute | solution.py:207
  62.9 9.0 %collective-permute-start.3 = (bf16[8,2,8,640]{3,2,1,0:T(8,128)(2,1)S(1)}, bf16[8,2,8,640]{3,2,1,0:T(8,128)(2,1)S(1)}, u32[]{:S(2)}, u32[]{:S(2)}) collective-permute-start(bf16[8,2,8,640]{3,2,1,0:T(8,128)(2,1)S(1)} %get-tuple-element.138), channel_id=1, source_target_pairs={{0,1},{1,2},{2,3},{4,5},{5,6},{6,7},{8,9},{9,10},{10,11},{12,13},{... | collective-permute-start | bytes 491528 | tf_op jit(solution)/shard_map/ppermute | solution.py:20
  66.7 24.9 %collective-permute-start.12 = (bf16[12,2,8,1792]{3,2,1,0:T(8,128)(2,1)S(1)}, bf16[12,2,8,1792]{3,2,1,0:T(8,128)(2,1)S(1)}, u32[]{:S(2)}, u32[]{:S(2)}) collective-permute-start(bf16[12,2,8,1792]{3,2,1,0:T(8,128)(2,1)S(1)} %copy-done.5), channel_id=1, source_target_pairs={{0,8},{4,12},{8,0},{12,4},{1,9},{5,13},{9,1},{13,5},{2,10},{6,14},... | collective-permute-start | bytes 2064392 | tf_op jit(solution)/shard_map/ppermute | solution.py:207
  68.1 27.0 %collective-permute-start.11 = (bf16[12,2,8,1792]{3,2,1,0:T(8,128)(2,1)S(1)}, bf16[12,2,8,1792]{3,2,1,0:T(8,128)(2,1)S(1)}, u32[]{:S(2)}, u32[]{:S(2)}) collective-permute-start(bf16[12,2,8,1792]{3,2,1,0:T(8,128)(2,1)S(1)} %copy-done.4), channel_id=1, source_target_pairs={{0,4},{4,8},{8,12},{12,0},{1,5},{5,9},{9,13},{13,1},{2,6},{6,10},{... | collective-permute-start | bytes 2064392 | tf_op jit(solution)/shard_map/ppermute | solution.py:207
  68.2 8.7 %collective-permute-start.4 = (bf16[8,2,8,640]{3,2,1,0:T(8,128)(2,1)S(1)}, bf16[8,2,8,640]{3,2,1,0:T(8,128)(2,1)S(1)}, u32[]{:S(2)}, u32[]{:S(2)}) collective-permute-start(bf16[8,2,8,640]{3,2,1,0:T(8,128)(2,1)S(1)} %get-tuple-element.139.refs_4_), channel_id=1, source_target_pairs={{1,0},{2,1},{3,2},{5,4},{6,5},{7,6},{9,8},{10,9},{11,10},{13,12},{... | collective-permute-start | bytes 491528 | tf_op jit(solution)/shard_map/ppermute | solution.py:20
  71.9 10.6 %collective-permute-start.8 = (bf16[8,2,8,1024]{3,2,1,0:T(8,128)(2,1)S(1)}, bf16[8,2,8,1024]{3,2,1,0:T(8,128)(2,1)S(1)}, u32[]{:S(2)}, u32[]{:S(2)}) collective-permute-start(bf16[8,2,8,1024]{3,2,1,0:T(8,128)(2,1)S(1)} %get-tuple-element.141), channel_id=1, source_target_pairs={{0,1},{1,2},{2,3},{4,5},{5,6},{6,7},{8,9},{9,10},{10,11},{12,13},{... | collective-permute-start | bytes 786440 | tf_op jit(solution)/shard_map/ppermute | solution.py:20
  76.9 10.0 %collective-permute-start.9 = (bf16[8,2,8,1024]{3,2,1,0:T(8,128)(2,1)S(1)}, bf16[8,2,8,1024]{3,2,1,0:T(8,128)(2,1)S(1)}, u32[]{:S(2)}, u32[]{:S(2)}) collective-permute-start(bf16[8,2,8,1024]{3,2,1,0:T(8,128)(2,1)S(1)} %get-tuple-element.142.refs_4_), channel_id=1, source_target_pairs={{1,0},{2,1},{3,2},{5,4},{6,5},{7,6},{9,8},{10,9},{11,10},{13,12},{... | collective-permute-start | bytes 786440 | tf_op jit(solution)/shard_map/ppermute | solution.py:20
  82.5 3.1 %collective-permute-start.21 = (bf16[16,2,8,128]{3,2,1,0:T(8,128)(2,1)S(1)}, bf16[16,2,8,128]{3,2,1,0:T(8,128)(2,1)S(1)}, u32[]{:S(2)}, u32[]{:S(2)}) collective-permute-start(bf16[16,2,8,128]{3,2,1,0:T(8,128)(2,1)S(1)} %slice.478), channel_id=1, source_target_pairs={{4,0},{8,4},{12,8},{5,1},{9,5},{13,9},{6,2},{10,6},{14,10},{7,3},{... | collective-permute-start | bytes 196616 | tf_op jit(solution)/shard_map/ppermute | solution.py:20
  85.6 12.9 %collective-permute-start.18 = (bf16[12,2,8,768]{3,2,1,0:T(8,128)(2,1)S(1)}, bf16[12,2,8,768]{3,2,1,0:T(8,128)(2,1)S(1)}, u32[]{:S(2)}, u32[]{:S(2)}) collective-permute-start(bf16[12,2,8,768]{3,2,1,0:T(8,128)(2,1)S(1)} %get-tuple-element.159), channel_id=1, source_target_pairs={{0,12},{4,0},{8,4},{12,8},{1,13},{5,1},{9,5},{13,9},{2,14},{6,2},{... | collective-permute-start | bytes 884744 | tf_op jit(solution)/shard_map/ppermute | solution.py:207
  86.9 18.7 %collective-permute-start.17 = (bf16[12,2,8,768]{3,2,1,0:T(8,128)(2,1)S(1)}, bf16[12,2,8,768]{3,2,1,0:T(8,128)(2,1)S(1)}, u32[]{:S(2)}, u32[]{:S(2)}) collective-permute-start(bf16[12,2,8,768]{3,2,1,0:T(8,128)(2,1)S(1)} %get-tuple-element.160), channel_id=1, source_target_pairs={{0,8},{4,12},{8,0},{12,4},{1,9},{5,13},{9,1},{13,5},{2,10},{6,14},... | collective-permute-start | bytes 884744 | tf_op jit(solution)/shard_map/ppermute | solution.py:207
  91.4 15.3 %collective-permute-start.16 = (bf16[12,2,8,768]{3,2,1,0:T(8,128)(2,1)S(1)}, bf16[12,2,8,768]{3,2,1,0:T(8,128)(2,1)S(1)}, u32[]{:S(2)}, u32[]{:S(2)}) collective-permute-start(bf16[12,2,8,768]{3,2,1,0:T(8,128)(2,1)S(1)} %get-tuple-element.161), channel_id=1, source_target_pairs={{0,4},{4,8},{8,12},{12,0},{1,5},{5,9},{9,13},{13,1},{2,6},{6,10},{... | collective-permute-start | bytes 884744 | tf_op jit(solution)/shard_map/ppermute | solution.py:207
  91.6 26.1 %collective-permute-start.10 = (bf16[16,2,8,128]{3,2,1,0:T(8,128)(2,1)S(1)}, bf16[16,2,8,128]{3,2,1,0:T(8,128)(2,1)S(1)}, u32[]{:S(2)}, u32[]{:S(2)}) collective-permute-start(bf16[16,2,8,128]{3,2,1,0:T(8,128)(2,1)S(1)} %slice.479), channel_id=1, source_target_pairs={{0,4},{4,8},{8,12},{1,5},{5,9},{9,13},{2,6},{6,10},{10,14},{3,7},{... | collective-permute-start | bytes 196616 | tf_op jit(solution)/shard_map/ppermute | solution.py:20
  97.3 27.7 %collective-permute-start.15 = (bf16[8,2,8,1792]{3,2,1,0:T(8,128)(2,1)S(1)}, bf16[8,2,8,1792]{3,2,1,0:T(8,128)(2,1)S(1)}, u32[]{:S(2)}, u32[]{:S(2)}) collective-permute-start(bf16[8,2,8,1792]{3,2,1,0:T(8,128)(2,1)S(1)} %get-tuple-element.145.refs_4_), channel_id=1, source_target_pairs={{1,0},{2,1},{3,2},{5,4},{6,5},{7,6},{9,8},{10,9},{11,10},{13,12},{... | collective-permute-start | bytes 1376264 | tf_op jit(solution)/shard_map/ppermute | solution.py:20
  108.3 9.4 %collective-permute-start.19 = (bf16[8,2,8,768]{3,2,1,0:T(8,128)(2,1)S(1)}, bf16[8,2,8,768]{3,2,1,0:T(8,128)(2,1)S(1)}, u32[]{:S(2)}, u32[]{:S(2)}) collective-permute-start(bf16[8,2,8,768]{3,2,1,0:T(8,128)(2,1)S(1)} %get-tuple-element.147), channel_id=1, source_target_pairs={{0,1},{1,2},{2,3},{4,5},{5,6},{6,7},{8,9},{9,10},{10,11},{12,13},{... | collective-permute-start | bytes 589832 | tf_op jit(solution)/shard_map/ppermute | solution.py:20
  111.8 7.6 %collective-permute-start.20 = (bf16[8,2,8,768]{3,2,1,0:T(8,128)(2,1)S(1)}, bf16[8,2,8,768]{3,2,1,0:T(8,128)(2,1)S(1)}, u32[]{:S(2)}, u32[]{:S(2)}) collective-permute-start(bf16[8,2,8,768]{3,2,1,0:T(8,128)(2,1)S(1)} %get-tuple-element.148), channel_id=1, source_target_pairs={{1,0},{2,1},{3,2},{5,4},{6,5},{7,6},{9,8},{10,9},{11,10},{13,12},{... | collective-permute-start | bytes 589832 | tf_op jit(solution)/shard_map/ppermute | solution.py:20
  113.1 11.7 %collective-permute-start.14 = (bf16[8,2,8,1792]{3,2,1,0:T(8,128)(2,1)S(1)}, bf16[8,2,8,1792]{3,2,1,0:T(8,128)(2,1)S(1)}, u32[]{:S(2)}, u32[]{:S(2)}) collective-permute-start(bf16[8,2,8,1792]{3,2,1,0:T(8,128)(2,1)S(1)} %get-tuple-element.144), channel_id=1, source_target_pairs={{0,1},{1,2},{2,3},{4,5},{5,6},{6,7},{8,9},{9,10},{10,11},{12,13},{... | collective-permute-start | bytes 1376264 | tf_op jit(solution)/shard_map/ppermute | solution.py:20
  (7 other events, 29.2 us)
